TPU v7x, 32 devices: a whole 2x2x4 slice. The times are simulated.
32 devices in a mesh: row: 4 (over x, core), col: 8 (over z, y).
Axes of the slice: x: 2, y: 2, z: 4, core: 2. Of those that a mesh axis runs over, the one named last changes fastest.
Arguments:
- embed: bfloat16 [1024, 768], P(('row', 'col'))
- beta: bfloat16 [1024], P(('row', 'col')), may hold values from 16 to 400
- block_mask: int32 [8, 8], P('row'), may hold values from 0 to 1, as said below
- counts: int32 [8], replicated, may hold values from 2 to 128
- probes: float32 [64, 1024], P(None, ('row', 'col')), may hold values from -6 to 6
Outputs:
- spectral: float32 [64, 1024], P(None, ('row', 'col'))
Inputs may be any that keep to these rules, and one draw needn't show every extreme that they name: `block_mask`: every diagonal entry is 1.
All inputs are finite; a program needn't handle non-finite values.
Results may differ from a plain program's by a relative error of at most 0.012.
The roundings to bfloat16 on the way count: a program that leaves them out, or rounds other values in their place, can miss the bound.
Values may be sent and summed in bfloat16 or wider, within the bound.
No kernel may reach another device: no remote copies, remote signals or barrier semaphores. Data moves between devices by JAX's collectives and lax.ppermute only.
A program may use at most 64 MiB of HBM per device.

v0:
```python
import jax
import jax.numpy as jnp
from jax import lax
from jax.sharding import PartitionSpec as P

ITERS = 2


def spread(shard, axis, root):
    mine = lax.axis_index(axis) == root
    return lax.psum(jnp.where(mine, shard, jnp.zeros_like(shard)), axis)


def own_piece(totals, col_ratio, n_row, row_index, col_index):
    shard_len = totals.shape[1] // n_row
    chosen = jnp.zeros_like(totals)
    for root_k in range(col_ratio):
        received = spread(totals, "col", col_ratio * row_index + root_k)
        chosen = jnp.where(col_index // n_row == root_k, received, chosen)
    return lax.dynamic_slice_in_dim(chosen, col_index % n_row * shard_len, shard_len, 1)


def body(embed, beta, block_mask, counts, probes):
    n_row = lax.axis_size("row")
    n_col = lax.axis_size("col")
    col_ratio = n_col // n_row
    row_index = lax.axis_index("row")
    col_index = lax.axis_index("col")
    shard_len, feat_width = embed.shape
    row_files = shard_len * n_col
    col_files = shard_len * n_row
    values = embed.astype(jnp.float32)
    unit_vec = (
        values * lax.rsqrt(jnp.mean(values * values, axis=1, keepdims=True) + 1e-06)
    ).astype(jnp.bfloat16)
    unit_rows, beta_rows = (
        lax.all_gather(unit_vec, "col", axis=0, tiled=True),
        lax.all_gather(beta, "col", axis=0, tiled=True),
    )
    half_pick = col_index % col_ratio
    col_seq = lax.iota(jnp.int32, col_files)
    unit_cols = spread(
        lax.dynamic_slice_in_dim(unit_rows, half_pick * col_files, col_files, 0),
        "row",
        col_index // col_ratio,
    )
    col_ids = col_index * col_files + col_seq
    gram_tile = lax.dot_general(
        unit_rows, unit_cols, (((1,), (1,)), ((), ())), preferred_element_type=jnp.float32
    )
    scores = gram_tile * (beta_rows.astype(jnp.float32) / feat_width)[:, None]
    row_blocks = block_mask.shape[0]
    blk_size = row_files // row_blocks
    col_block = col_ids // blk_size
    col_live = col_ids % blk_size < jnp.take(counts, col_block, axis=0)
    mask_cols = jnp.take(block_mask, col_block, axis=1) == 1
    block_wide = jnp.broadcast_to(mask_cols[:, None, :], (row_blocks, blk_size, col_files)).reshape(
        row_files, col_files
    )
    row_ids = row_index * row_files + lax.iota(jnp.int32, row_files)
    allowed = block_wide & col_live[None, :] & (row_ids[:, None] != col_ids[None, :])
    masked = jnp.where(allowed, scores, -1e30)
    local_top = jnp.max(masked, axis=1)
    row_top = lax.pmax(local_top, "col")
    row_mass = lax.psum(
        jnp.sum(jnp.where(allowed, jnp.exp(masked - row_top[:, None]), 0.0), axis=1), "col"
    )
    weights = jnp.where(allowed, jnp.exp(masked - row_top[:, None]) / row_mass[:, None], 0.0)
    col_mass = lax.psum(jnp.sum(weights, axis=0), "row")
    own_mass = own_piece(col_mass[None, :], col_ratio, n_row, row_index, col_index)[0]
    inv_root = lax.rsqrt((1.0 + own_mass) * 0.5)
    affinity = weights.astype(jnp.bfloat16)
    probe_state = probes
    for sweep in range(ITERS):
        scaled = (probe_state * inv_root[None, :]).astype(jnp.bfloat16)
        probe_rows = lax.all_gather(scaled, "col", axis=1, tiled=True)
        probe_cols = spread(
            lax.dynamic_slice_in_dim(probe_rows, half_pick * col_files, col_files, 1),
            "row",
            col_index // col_ratio,
        )
        row_part = lax.dot_general(
            probe_cols, affinity, (((1,), (1,)), ((), ())), preferred_element_type=jnp.float32
        )
        col_part = jnp.dot(probe_rows, affinity, preferred_element_type=jnp.float32)
        own_rows = lax.psum_scatter(
            row_part.astype(jnp.bfloat16), "col", scatter_dimension=1, tiled=True
        ).astype(jnp.float32)
        col_total = lax.psum(col_part, "row")
        own_cols = own_piece(col_total, col_ratio, n_row, row_index, col_index)
        probe_state = (own_rows + own_cols) * (0.5 * inv_root)[None, :]
    return probe_state


def solution(mesh):
    placed = (
        P(("row", "col"), None),
        P(("row", "col")),
        P("row", None),
        P(),
        P(None, ("row", "col")),
    )
    return jax.shard_map(
        body, mesh=mesh, in_specs=placed, out_specs=P(None, ("row", "col")), check_vma=False
    )
```

profile of v0, /device:TPU:0, one launch (start us, length us, event | category | flops | bytes accessed | tf_op | source)
XLA Modules:
  0.0 495.1 jit_solution(6957773946014642195)
XLA Ops:
  6.5 0.8 copy-done
  7.5 32.7 %all_gather.12 = bf16[256,768]{1,0:T(8,128)(2,1)S(1)} all-gather(bf16[32,768]{1,0:T(8,128)(2,1)S(1)} %fusion.2), channel_id=1, replica_groups=mesh['row'=4,'col'=8] {'col'}, dimensions={0}, use_global_device_ids=true | all-gather | bytes 442368 | tf_op jit(solution)/shard_map/all_gather | solution.py:37
  40.3 0.7 dynamic-slice_select_fusion
  41.2 0.6 copy-done.1
  41.8 0.7 fusion.21
  42.5 0.7 copy-done.3
  43.3 0.6 gather_fusion
  44.3 0.6 copy-done.5
  46.2 0.6 copy-done.4
  47.0 21.5 %all-reduce = bf16[256]{0:T(256)(128)(2,1)S(1)} all-reduce(bf16[256]{0:T(256)(128)(2,1)S(1)} %dynamic-update-slice), channel_id=1, replica_groups=mesh['row'=4,'col'=8] {'col'}, use_global_device_ids=true, to_apply=%add | all-reduce | flops 256 | bytes 1024
  68.5 5.1 %fusion.12 = pred[128]{0:T(512)(128)(4,1)S(1)} fusion(s32[]{:T(128)} %bitcast.3, s32[]{:T(128)} %bitcast.4, s32[]{:T(128)} %bitcast.5, s32[]{:T(128)} %bitcast.6, s32[]{:T(128)} %bitcast.7, s32[]{:T(128)} %bitcast.8, s32[]{:T(128)} %bitcast.9, s32[]{:T(128)} %bitcast.10, s32[]{:T(128)S(6)} %mul.86), kind=kLoop, calls=%fused_computation.62 | loop fusion | flops 7808 | bytes 164 | tf_op jit(solution)/shard_map/lt | solution.py:55
  74.0 1.2 fusion.22
  75.2 21.3 %pmax.7 = f32[256]{0:T(256)S(1)} all-reduce(f32[256]{0:T(256)S(1)} %get-tuple-element.29), channel_id=1, replica_groups=mesh['row'=4,'col'=8] {'col'}, use_global_device_ids=true, to_apply=%region_3.4 | all-reduce | flops 256 | bytes 2048 | tf_op jit(solution)/shard_map/pmax | solution.py:64
  96.7 17.1 %psum.92 = f32[256]{0:T(256)S(1)} all-reduce(f32[256]{0:T(256)S(1)} %select_reduce_fusion), channel_id=1, replica_groups=mesh['row'=4,'col'=8] {'col'}, use_global_device_ids=true, to_apply=%region_5.6 | all-reduce | flops 256 | bytes 2048 | tf_op jit(solution)/shard_map/psum | solution.py:65
  114.0 5.9 %psum.93 = f32[128]{0:T(128)S(1)} all-reduce(f32[128]{0:T(128)S(1)} %get-tuple-element.13), channel_id=1, replica_groups=mesh['row'=4,'col'=8] {'row'}, use_global_device_ids=true, to_apply=%region_7.8 | all-reduce | flops 128 | bytes 1024 | tf_op jit(solution)/shard_map/psum | solution.py:69
  119.9 19.1 %all-reduce.3 = (f32[1,128]{1,0:T(1,128)S(1)}, f32[1,128]{1,0:T(1,128)S(1)}) all-reduce(f32[1,128]{1,0:T(1,128)S(1)} %get-tuple-element.20, f32[1,128]{1,0:T(1,128)S(1)} %get-tuple-element.19), channel_id=1, replica_groups=mesh['row'=4,'col'=8] {'col'}, use_global_device_ids=true, to_apply=%region_8.9 | all-reduce | flops 256 | bytes 2048 | tf_op jit(solution)/shard_map/psum | solution.py:11
  139.2 30.5 %all_gather.14 = bf16[64,256]{0,1:T(8,128)(2,1)S(1)} all-gather(bf16[64,32]{0,1:T(8,128)(2,1)S(1)} %multiply_convert_fusion), channel_id=1, replica_groups=mesh['row'=4,'col'=8] {'col'}, dimensions={1}, use_global_device_ids=true | all-gather | bytes 36864 | tf_op jit(solution)/shard_map/all_gather | solution.py:76
  169.7 10.3 %psum.96 = bf16[64,128]{0,1:T(8,128)(2,1)S(1)} all-reduce(bf16[64,128]{0,1:T(8,128)(2,1)S(1)} %dynamic-slice_select_fusion.2), channel_id=1, replica_groups=mesh['row'=4,'col'=8] {'row'}, use_global_device_ids=true, to_apply=%region_10.11 | all-reduce | flops 8192 | bytes 32768 | tf_op jit(solution)/shard_map/psum | solution.py:11
  180.1 0.8 convolution_convert_fusion.1
  181.0 10.7 %psum.97 = f32[64,128]{0,1:T(8,128)S(1)} all-reduce(f32[64,128]{0,1:T(8,128)S(1)} %fusion.23), channel_id=1, replica_groups=mesh['row'=4,'col'=8] {'row'}, use_global_device_ids=true, to_apply=%region_12.13 | all-reduce | flops 8192 | bytes 65536 | tf_op jit(solution)/shard_map/psum | solution.py:89
  191.8 0.7 broadcast_select_fusion.2
  192.5 46.2 %reduce-scatter.3.cloned.1.call-done = bf16[64,32]{0,1:T(8,128)(2,1)} async-done(((bf16[64,256]{0,1:T(8,128)(2,1)}), bf16[64,32]{0,1:T(8,128)(2,1)}) %reduce-scatter.3.cloned.1.call-update) | async-done | bytes 4112 | tf_op jit(solution)/shard_map/reduce_scatter | solution.py:86
  238.7 72.8 %all-reduce.12.cloned.1.call-done = (f32[64,128]{0,1:T(8,128)}, f32[64,128]{0,1:T(8,128)}) async-done(((f32[64,128]{0,1:T(8,128)}, f32[64,128]{0,1:T(8,128)}), (f32[64,128]{0,1:T(8,128)}, f32[64,128]{0,1:T(8,128)})) %all-reduce.12.cloned.1.call-update) | async-done | bytes 65552 | tf_op jit(solution)/shard_map/psum | solution.py:11
  311.5 0.8 fusion.9
  312.3 30.5 %all_gather.15 = bf16[64,256]{0,1:T(8,128)(2,1)S(1)} all-gather(bf16[64,32]{0,1:T(8,128)(2,1)S(1)} %fusion.9), channel_id=1, replica_groups=mesh['row'=4,'col'=8] {'col'}, dimensions={1}, use_global_device_ids=true | all-gather | bytes 36864 | tf_op jit(solution)/shard_map/all_gather | solution.py:76
  343.0 10.3 %psum.100 = bf16[64,128]{0,1:T(8,128)(2,1)S(1)} all-reduce(bf16[64,128]{0,1:T(8,128)(2,1)S(1)} %dynamic-slice_select_fusion.1), channel_id=1, replica_groups=mesh['row'=4,'col'=8] {'row'}, use_global_device_ids=true, to_apply=%region_15.16 | all-reduce | flops 8192 | bytes 32768 | tf_op jit(solution)/shard_map/psum | solution.py:11
  353.3 0.8 convolution_convert_fusion
  354.2 11.8 %psum.101 = f32[64,128]{0,1:T(8,128)S(1)} all-reduce(f32[64,128]{0,1:T(8,128)S(1)} %fusion.24), channel_id=1, replica_groups=mesh['row'=4,'col'=8] {'row'}, use_global_device_ids=true, to_apply=%region_17.18 | all-reduce | flops 8192 | bytes 65536 | tf_op jit(solution)/shard_map/psum | solution.py:89
  366.0 0.7 broadcast_select_fusion.1
  366.7 48.3 %reduce-scatter.5.cloned.1.call-done = bf16[64,32]{0,1:T(8,128)(2,1)} async-done(((bf16[64,256]{0,1:T(8,128)(2,1)}), bf16[64,32]{0,1:T(8,128)(2,1)}) %reduce-scatter.5.cloned.1.call-update) | async-done | bytes 4112 | tf_op jit(solution)/shard_map/reduce_scatter | solution.py:86
  415.0 72.3 %all-reduce.10.cloned.1.call-done = (f32[64,128]{0,1:T(8,128)}, f32[64,128]{0,1:T(8,128)}) async-done(((f32[64,128]{0,1:T(8,128)}, f32[64,128]{0,1:T(8,128)}), (f32[64,128]{0,1:T(8,128)}, f32[64,128]{0,1:T(8,128)})) %all-reduce.10.cloned.1.call-update) | async-done | bytes 65552 | tf_op jit(solution)/shard_map/psum | solution.py:11
  487.2 1.4 fusion.5
  (45 shorter events, 2.8 us)
Async XLA Ops:
  6.5 0.8 copy-start
  6.5 67.5 %all-reduce.8.cloned.1.call-start = ((), (), s32[]{:S(2)}) async-start(), calls=%async_computation.2 | async-start | bytes 393216 | tf_op jit(solution)/shard_map/psum | solution.py:11
  41.0 197.7 %reduce-scatter.3.cloned.1.call-start = ((), (), s32[]{:S(2)}) async-start(), calls=%async_computation.3 | async-start | bytes 73728 | tf_op jit(solution)/shard_map/reduce_scatter | solution.py:86
  41.2 0.7 copy-start.1
  42.5 0.7 copy-start.3
  44.2 0.7 copy-start.5
  46.1 0.7 copy-start.4
  114.0 25.1 %copy-start.2 = (f32[64,32]{0,1:T(8,128)S(1)}, f32[64,32]{0,1:T(8,128)}, u32[]{:S(2)}) copy-start(f32[64,32]{0,1:T(8,128)} %param.9) | copy-start | bytes 24580
  181.0 130.5 %all-reduce.12.cloned.1.call-start = ((), (), s32[]{:S(2)}) async-start(), calls=%async_computation.6 | async-start | bytes 262144 | tf_op jit(solution)/shard_map/psum | solution.py:11
  192.4 222.5 %reduce-scatter.5.cloned.1.call-start = ((), (), s32[]{:S(2)}) async-start(), calls=%async_computation.4 | async-start | bytes 73728 | tf_op jit(solution)/shard_map/reduce_scatter | solution.py:86
  354.1 133.1 %all-reduce.10.cloned.1.call-start = ((), (), s32[]{:S(2)}) async-start(), calls=%async_computation.5 | async-start | bytes 262144 | tf_op jit(solution)/shard_map/psum | solution.py:11
Sparse Core Ops, SparseCore 0:
  41.1 32.8 all-reduce.7
  181.1 57.5 reduce-scatter.2
  242.6 68.8 all-reduce.11
  354.3 60.6 reduce-scatter.4
  418.3 68.8 all-reduce.9
where the time goes:
time: 496 us; the launch traced here: 495 us
  waiting for transfers between devices  240 us (48%)
  blocking collectives  222 us (45%)
  between operations  14 us (3%)
  other arithmetic  10.2 us (2%)
  local copies, waits for them, and re-layouts  5.8 us (1%)
    psum x3, waiting for transfers between devices, spread(): return lax.psum(jnp.where(mine, shard, jnp.zeros_like(shard)), axis)  145 us
    reduce_scatter x2, waiting for transfers between devices, body(): lax.psum_scatter(row_part.astype(jnp.bfloat16), 'col', scatter_dimension=...  94.5 us
    all_gather x2, blocking collectives, body(): probe_rows = lax.all_gather(scaled, 'col', axis=1, tiled=True)  61 us
    psum x3, blocking collectives, spread(): return lax.psum(jnp.where(mine, shard, jnp.zeros_like(shard)), axis)  39.7 us
    all_gather x1, blocking collectives, body(): lax.all_gather(unit_vec, 'col', axis=0, tiled=True)  32.7 us
    psum x2, blocking collectives, body(): col_total = lax.psum(col_part, 'row')  22.5 us
    unnamed x1, blocking collectives  21.5 us
    pmax x1, blocking collectives, body(): row_top = lax.pmax(local_top, 'col')  21.3 us
  transfers between devices with their start and end apart: 5, of which 5 were waited for; matrix products, arithmetic and copies ran while one was open for 2% of the time, Pallas kernels for 0%

commit v1 on v0

--- a/solution.py
+++ b/solution.py
@@ -73,7 +73,26 @@
     probe_state = probes
     for sweep in range(ITERS):
         scaled = (probe_state * inv_root[None, :]).astype(jnp.bfloat16)
-        probe_rows = lax.all_gather(scaled, "col", axis=1, tiled=True)
+        devices, index, rows = (lax.axis_size("col"), lax.axis_index("col"), scaled.shape[1])
+        forward = [(i, (i + 1) % devices) for i in range(devices)]
+        left = [(i, (i - 1) % devices) for i in range(devices)]
+        result = jnp.zeros(
+            (*scaled.shape[:1], devices * rows, *scaled.shape[1 + 1 :]), scaled.dtype
+        )
+        result = lax.dynamic_update_slice_in_dim(result, scaled, index * rows, axis=1)
+        from_left = from_right = scaled
+        halfway = devices // 2
+        for turn in range(1, halfway + 1):
+            from_left = lax.ppermute(from_left, "col", forward)
+            result = lax.dynamic_update_slice_in_dim(
+                result, from_left, (index - turn) % devices * rows, axis=1
+            )
+            if turn < devices - halfway:
+                from_right = lax.ppermute(from_right, "col", left)
+                result = lax.dynamic_update_slice_in_dim(
+                    result, from_right, (index + turn) % devices * rows, axis=1
+                )
+        probe_rows = result
         probe_cols = spread(
             lax.dynamic_slice_in_dim(probe_rows, half_pick * col_files, col_files, 1),
             "row",

time: 496 us -> 485 us (0.978)
  blocking collectives: 222 us -> 160 us
  starting transfers between devices: 0.17 us -> 28.6 us
  waiting for transfers between devices: 240 us -> 260 us
    all_gather x2 -> x0, blocking collectives: 61 us -> none  [body(): probe_rows = lax.all_gather(scaled, 'col', axis=1, tiled=True)]
    ppermute x0 -> x14, starting transfers between devices: none -> 28.4 us  [the longest x6 27.5 us: body(): from_right = lax.ppermute(from_right, 'col', left)]
    ppermute x0 -> x14, waiting for transfers between devices: none -> 22.4 us  [the longest x8 22.4 us: body(): from_left = lax.ppermute(from_left, 'col', forward)]
  transfers between devices with their start and end apart: 5 -> 19, of which waited for: 5 -> 13; matrix products, arithmetic and copies ran while one was open for 2% -> 2% of each run, Pallas kernels for 0% -> 0%
where the time goes in v1:
time: 485 us; the launch traced here: 484 us
  waiting for transfers between devices  260 us (54%)
  blocking collectives  160 us (33%)
  starting transfers between devices  28.6 us (6%)
  between operations  14.1 us (3%)
  other arithmetic  10.2 us (2%)
  local copies, waits for them, and re-layouts  7.31 us (2%)
    psum x3, waiting for transfers between devices, spread(): return lax.psum(jnp.where(mine, shard, jnp.zeros_like(shard)), axis)  145 us
    reduce_scatter x2, waiting for transfers between devices, body(): lax.psum_scatter(row_part.astype(jnp.bfloat16), 'col', scatter_dimension=...  92.6 us
    psum x3, blocking collectives, spread(): return lax.psum(jnp.where(mine, shard, jnp.zeros_like(shard)), axis)  39.7 us
    all_gather x1, blocking collectives, body(): lax.all_gather(unit_vec, 'col', axis=0, tiled=True)  32.7 us
    ppermute x6, starting transfers between devices, body(): from_right = lax.ppermute(from_right, 'col', left)  27.5 us
    ppermute x8, waiting for transfers between devices, body(): from_left = lax.ppermute(from_left, 'col', forward)  22.4 us
    psum x2, blocking collectives, body(): col_total = lax.psum(col_part, 'row')  22.1 us
    unnamed x1, blocking collectives  21.5 us
  transfers between devices with their start and end apart: 19, of which 13 were waited for; matrix products, arithmetic and copies ran while one was open for 2% of the time, Pallas kernels for 0%

profile of v1, /device:TPU:0, one launch (start us, length us, event | category | flops | bytes accessed | tf_op | source)
XLA Modules:
  0.0 484.2 jit_solution(14853227262513990994)
XLA Ops:
  7.5 32.7 %all_gather.6 = bf16[256,768]{1,0:T(8,128)(2,1)S(1)} all-gather(bf16[32,768]{1,0:T(8,128)(2,1)S(1)} %fusion.2), channel_id=1, replica_groups=mesh['row'=4,'col'=8] {'col'}, dimensions={0}, use_global_device_ids=true | all-gather | bytes 442368 | tf_op jit(solution)/shard_map/all_gather | solution.py:37
  47.0 21.5 %all-reduce = bf16[256]{0:T(256)(128)(2,1)S(1)} all-reduce(bf16[256]{0:T(256)(128)(2,1)S(1)} %dynamic-update-slice), channel_id=1, replica_groups=mesh['row'=4,'col'=8] {'col'}, use_global_device_ids=true, to_apply=%add | all-reduce | flops 256 | bytes 1024
  68.5 5.1 %fusion.12 = pred[128]{0:T(512)(128)(4,1)S(1)} fusion(s32[]{:T(128)} %bitcast.3, s32[]{:T(128)} %bitcast.4, s32[]{:T(128)} %bitcast.5, s32[]{:T(128)} %bitcast.6, s32[]{:T(128)} %bitcast.7, s32[]{:T(128)} %bitcast.8, s32[]{:T(128)} %bitcast.9, s32[]{:T(128)} %bitcast.10, s32[]{:T(128)S(6)} %mul.118), kind=kLoop, calls=%fused_computation.78 | loop fusion | flops 7808 | bytes 164 | tf_op jit(solution)/shard_map/lt | solution.py:55
  74.0 1.2 fusion.23
  75.2 21.4 %pmax.7 = f32[256]{0:T(256)S(1)} all-reduce(f32[256]{0:T(256)S(1)} %get-tuple-element.33), channel_id=1, replica_groups=mesh['row'=4,'col'=8] {'col'}, use_global_device_ids=true, to_apply=%region_3.4 | all-reduce | flops 256 | bytes 2048 | tf_op jit(solution)/shard_map/pmax | solution.py:64
  96.7 17.1 %psum.92 = f32[256]{0:T(256)S(1)} all-reduce(f32[256]{0:T(256)S(1)} %select_reduce_fusion), channel_id=1, replica_groups=mesh['row'=4,'col'=8] {'col'}, use_global_device_ids=true, to_apply=%region_5.6 | all-reduce | flops 256 | bytes 2048 | tf_op jit(solution)/shard_map/psum | solution.py:65
  114.0 5.9 %psum.93 = f32[128]{0:T(128)S(1)} all-reduce(f32[128]{0:T(128)S(1)} %get-tuple-element.17), channel_id=1, replica_groups=mesh['row'=4,'col'=8] {'row'}, use_global_device_ids=true, to_apply=%region_7.8 | all-reduce | flops 128 | bytes 1024 | tf_op jit(solution)/shard_map/psum | solution.py:69
  119.9 19.1 %all-reduce.3 = (f32[1,128]{1,0:T(1,128)S(1)}, f32[1,128]{1,0:T(1,128)S(1)}) all-reduce(f32[1,128]{1,0:T(1,128)S(1)} %get-tuple-element.24, f32[1,128]{1,0:T(1,128)S(1)} %get-tuple-element.23), channel_id=1, replica_groups=mesh['row'=4,'col'=8] {'col'}, use_global_device_ids=true, to_apply=%region_8.9 | all-reduce | flops 256 | bytes 2048 | tf_op jit(solution)/shard_map/psum | solution.py:11
  139.9 4.7 collective-permute-start.1
  144.6 1.6 collective-permute-done
  146.3 4.7 collective-permute-start.3
  151.0 1.6 collective-permute-done.2
  152.6 4.7 collective-permute-start.5
  157.3 1.6 collective-permute-done.4
  159.0 6.3 %collective-permute-done.6 = bf16[64,32]{0,1:T(8,128)(2,1)S(1)} collective-permute-done((bf16[64,32]{0,1:T(8,128)(2,1)S(1)}, bf16[64,32]{0,1:T(8,128)(2,1)S(1)}, u32[]{:S(2)}, u32[]{:S(2)}) %collective-permute-start.6) | collective-permute-done | bytes 4128 | tf_op jit(solution)/shard_map/ppermute | solution.py:86
  165.3 10.3 %psum.96 = bf16[64,128]{0,1:T(8,128)(2,1)S(1)} all-reduce(bf16[64,128]{0,1:T(8,128)(2,1)S(1)} %dynamic-slice_select_fusion.2), channel_id=1, replica_groups=mesh['row'=4,'col'=8] {'row'}, use_global_device_ids=true, to_apply=%region_10.11 | all-reduce | flops 8192 | bytes 32768 | tf_op jit(solution)/shard_map/psum | solution.py:11
  176.7 10.7 %psum.97 = f32[64,128]{0,1:T(8,128)S(1)} all-reduce(f32[64,128]{0,1:T(8,128)S(1)} %fusion.24), channel_id=1, replica_groups=mesh['row'=4,'col'=8] {'row'}, use_global_device_ids=true, to_apply=%region_12.13 | all-reduce | flops 8192 | bytes 65536 | tf_op jit(solution)/shard_map/psum | solution.py:108
  188.1 46.0 %reduce-scatter.3.cloned.1.call-done = bf16[64,32]{0,1:T(8,128)(2,1)} async-done(((bf16[64,256]{0,1:T(8,128)(2,1)}), bf16[64,32]{0,1:T(8,128)(2,1)}) %reduce-scatter.3.cloned.1.call-update) | async-done | bytes 4112 | tf_op jit(solution)/shard_map/reduce_scatter | solution.py:105
  234.1 72.8 %all-reduce.12.cloned.1.call-done = (f32[64,128]{0,1:T(8,128)}, f32[64,128]{0,1:T(8,128)}) async-done(((f32[64,128]{0,1:T(8,128)}, f32[64,128]{0,1:T(8,128)}), (f32[64,128]{0,1:T(8,128)}, f32[64,128]{0,1:T(8,128)})) %all-reduce.12.cloned.1.call-update) | async-done | bytes 65552 | tf_op jit(solution)/shard_map/psum | solution.py:11
  308.4 0.8 collective-permute-start.7
  309.3 3.9 collective-permute-start.8
  313.2 1.6 collective-permute-done.7
  314.8 4.7 collective-permute-start.10
  319.6 1.6 collective-permute-done.9
  321.2 4.7 collective-permute-start.12
  325.9 1.7 collective-permute-done.11
  327.6 6.3 %collective-permute-done.13 = bf16[64,32]{0,1:T(8,128)(2,1)S(1)} collective-permute-done((bf16[64,32]{0,1:T(8,128)(2,1)S(1)}, bf16[64,32]{0,1:T(8,128)(2,1)S(1)}, u32[]{:S(2)}, u32[]{:S(2)}) %collective-permute-start.13) | collective-permute-done | bytes 4128 | tf_op jit(solution)/shard_map/ppermute | solution.py:86
  334.1 10.3 %psum.100 = bf16[64,128]{0,1:T(8,128)(2,1)S(1)} all-reduce(bf16[64,128]{0,1:T(8,128)(2,1)S(1)} %dynamic-slice_select_fusion.1), channel_id=1, replica_groups=mesh['row'=4,'col'=8] {'row'}, use_global_device_ids=true, to_apply=%region_15.16 | all-reduce | flops 8192 | bytes 32768 | tf_op jit(solution)/shard_map/psum | solution.py:11
  345.3 11.4 %psum.101 = f32[64,128]{0,1:T(8,128)S(1)} all-reduce(f32[64,128]{0,1:T(8,128)S(1)} %fusion.25), channel_id=1, replica_groups=mesh['row'=4,'col'=8] {'row'}, use_global_device_ids=true, to_apply=%region_17.18 | all-reduce | flops 8192 | bytes 65536 | tf_op jit(solution)/shard_map/psum | solution.py:108
  357.4 46.6 %reduce-scatter.5.cloned.1.call-done = bf16[64,32]{0,1:T(8,128)(2,1)} async-done(((bf16[64,256]{0,1:T(8,128)(2,1)}), bf16[64,32]{0,1:T(8,128)(2,1)}) %reduce-scatter.5.cloned.1.call-update) | async-done | bytes 4112 | tf_op jit(solution)/shard_map/reduce_scatter | solution.py:105
  404.0 72.3 %all-reduce.10.cloned.1.call-done = (f32[64,128]{0,1:T(8,128)}, f32[64,128]{0,1:T(8,128)}) async-done(((f32[64,128]{0,1:T(8,128)}, f32[64,128]{0,1:T(8,128)}), (f32[64,128]{0,1:T(8,128)}, f32[64,128]{0,1:T(8,128)})) %all-reduce.10.cloned.1.call-update) | async-done | bytes 65552 | tf_op jit(solution)/shard_map/psum | solution.py:11
  476.3 1.4 fusion.5
  (89 shorter events, 13.6 us)
Async XLA Ops:
  6.5 0.8 copy-start
  6.5 67.4 %all-reduce.8.cloned.1.call-start = ((), (), s32[]{:S(2)}) async-start(), calls=%async_computation.2 | async-start | bytes 393216 | tf_op jit(solution)/shard_map/psum | solution.py:11
  41.0 193.1 %reduce-scatter.3.cloned.1.call-start = ((), (), s32[]{:S(2)}) async-start(), calls=%async_computation.3 | async-start | bytes 73728 | tf_op jit(solution)/shard_map/reduce_scatter | solution.py:105
  41.2 0.7 copy-start.1
  42.5 0.7 copy-start.4
  44.3 0.7 copy-start.6
  46.2 0.7 copy-start.5
  139.1 0.7 copy-start.2
  139.9 6.3 %collective-permute-start = (bf16[64,32]{0,1:T(8,128)(2,1)S(1)}, bf16[64,32]{0,1:T(8,128)(2,1)S(1)}, u32[]{:S(2)}, u32[]{:S(2)}) collective-permute-start(bf16[64,32]{0,1:T(8,128)(2,1)S(1)} %get-tuple-element.16), channel_id=1, source_target_pairs={{0,1},{1,2},{2,3},{3,4},{4,5},{5,6},{6,7},{7,0},{8,9},{9,10},{10,1... | collective-permute-start | bytes 12296 | tf_op jit(solution)/shard_map/ppermute | solution.py:86
  139.9 6.3 %collective-permute-start.1 = (bf16[64,32]{0,1:T(8,128)(2,1)S(1)}, bf16[64,32]{0,1:T(8,128)(2,1)S(1)}, u32[]{:S(2)}, u32[]{:S(2)}) collective-permute-start(bf16[64,32]{0,1:T(8,128)(2,1)S(1)} %get-tuple-element.16), channel_id=1, source_target_pairs={{0,7},{1,0},{2,1},{3,2},{4,3},{5,4},{6,5},{7,6},{8,15},{9,8},{10,9... | collective-permute-start | bytes 12296 | tf_op jit(solution)/shard_map/ppermute | solution.py:91
  146.3 6.3 %collective-permute-start.2 = (bf16[64,32]{0,1:T(8,128)(2,1)S(1)}, bf16[64,32]{0,1:T(8,128)(2,1)S(1)}, u32[]{:S(2)}, u32[]{:S(2)}) collective-permute-start(bf16[64,32]{0,1:T(8,128)(2,1)S(1)} %collective-permute-done), channel_id=1, source_target_pairs={{0,1},{1,2},{2,3},{3,4},{4,5},{5,6},{6,7},{7,0},{8,9},{9,10},{10,1... | collective-permute-start | bytes 12296 | tf_op jit(solution)/shard_map/ppermute | solution.py:86
  146.3 6.3 %collective-permute-start.3 = (bf16[64,32]{0,1:T(8,128)(2,1)S(1)}, bf16[64,32]{0,1:T(8,128)(2,1)S(1)}, u32[]{:S(2)}, u32[]{:S(2)}) collective-permute-start(bf16[64,32]{0,1:T(8,128)(2,1)S(1)} %collective-permute-done.1), channel_id=1, source_target_pairs={{0,7},{1,0},{2,1},{3,2},{4,3},{5,4},{6,5},{7,6},{8,15},{9,8},{10,9... | collective-permute-start | bytes 12296 | tf_op jit(solution)/shard_map/ppermute | solution.py:91
  152.6 6.3 %collective-permute-start.4 = (bf16[64,32]{0,1:T(8,128)(2,1)S(1)}, bf16[64,32]{0,1:T(8,128)(2,1)S(1)}, u32[]{:S(2)}, u32[]{:S(2)}) collective-permute-start(bf16[64,32]{0,1:T(8,128)(2,1)S(1)} %collective-permute-done.2), channel_id=1, source_target_pairs={{0,1},{1,2},{2,3},{3,4},{4,5},{5,6},{6,7},{7,0},{8,9},{9,10},{10,1... | collective-permute-start | bytes 12296 | tf_op jit(solution)/shard_map/ppermute | solution.py:86
  152.6 6.4 %collective-permute-start.5 = (bf16[64,32]{0,1:T(8,128)(2,1)S(1)}, bf16[64,32]{0,1:T(8,128)(2,1)S(1)}, u32[]{:S(2)}, u32[]{:S(2)}) collective-permute-start(bf16[64,32]{0,1:T(8,128)(2,1)S(1)} %collective-permute-done.3), channel_id=1, source_target_pairs={{0,7},{1,0},{2,1},{3,2},{4,3},{5,4},{6,5},{7,6},{8,15},{9,8},{10,9... | collective-permute-start | bytes 12296 | tf_op jit(solution)/shard_map/ppermute | solution.py:91
  159.0 6.3 %collective-permute-start.6 = (bf16[64,32]{0,1:T(8,128)(2,1)S(1)}, bf16[64,32]{0,1:T(8,128)(2,1)S(1)}, u32[]{:S(2)}, u32[]{:S(2)}) collective-permute-start(bf16[64,32]{0,1:T(8,128)(2,1)S(1)} %collective-permute-done.4), channel_id=1, source_target_pairs={{0,1},{1,2},{2,3},{3,4},{4,5},{5,6},{6,7},{7,0},{8,9},{9,10},{10,1... | collective-permute-start | bytes 12296 | tf_op jit(solution)/shard_map/ppermute | solution.py:86
  176.6 130.3 %all-reduce.12.cloned.1.call-start = ((), (), s32[]{:S(2)}) async-start(), calls=%async_computation.6 | async-start | bytes 262144 | tf_op jit(solution)/shard_map/psum | solution.py:11
  188.1 215.9 %reduce-scatter.5.cloned.1.call-start = ((), (), s32[]{:S(2)}) async-start(), calls=%async_computation.4 | async-start | bytes 73728 | tf_op jit(solution)/shard_map/reduce_scatter | solution.py:105
  306.9 0.7 copy-start.3
  308.4 6.4 %collective-permute-start.7 = (bf16[64,32]{0,1:T(8,128)(2,1)S(1)}, bf16[64,32]{0,1:T(8,128)(2,1)S(1)}, u32[]{:S(2)}, u32[]{:S(2)}) collective-permute-start(bf16[64,32]{0,1:T(8,128)(2,1)S(1)} %get-tuple-element.12), channel_id=1, source_target_pairs={{0,1},{1,2},{2,3},{3,4},{4,5},{5,6},{6,7},{7,0},{8,9},{9,10},{10,1... | collective-permute-start | bytes 12296 | tf_op jit(solution)/shard_map/ppermute | solution.py:86
  309.3 5.6 %collective-permute-start.8 = (bf16[64,32]{0,1:T(8,128)(2,1)S(1)}, bf16[64,32]{0,1:T(8,128)(2,1)S(1)}, u32[]{:S(2)}, u32[]{:S(2)}) collective-permute-start(bf16[64,32]{0,1:T(8,128)(2,1)S(1)} %get-tuple-element.12), channel_id=1, source_target_pairs={{0,7},{1,0},{2,1},{3,2},{4,3},{5,4},{6,5},{7,6},{8,15},{9,8},{10,9... | collective-permute-start | bytes 12296 | tf_op jit(solution)/shard_map/ppermute | solution.py:91
  314.8 6.3 %collective-permute-start.9 = (bf16[64,32]{0,1:T(8,128)(2,1)S(1)}, bf16[64,32]{0,1:T(8,128)(2,1)S(1)}, u32[]{:S(2)}, u32[]{:S(2)}) collective-permute-start(bf16[64,32]{0,1:T(8,128)(2,1)S(1)} %collective-permute-done.7), channel_id=1, source_target_pairs={{0,1},{1,2},{2,3},{3,4},{4,5},{5,6},{6,7},{7,0},{8,9},{9,10},{10,1... | collective-permute-start | bytes 12296 | tf_op jit(solution)/shard_map/ppermute | solution.py:86
  314.8 6.3 %collective-permute-start.10 = (bf16[64,32]{0,1:T(8,128)(2,1)S(1)}, bf16[64,32]{0,1:T(8,128)(2,1)S(1)}, u32[]{:S(2)}, u32[]{:S(2)}) collective-permute-start(bf16[64,32]{0,1:T(8,128)(2,1)S(1)} %collective-permute-done.8), channel_id=1, source_target_pairs={{0,7},{1,0},{2,1},{3,2},{4,3},{5,4},{6,5},{7,6},{8,15},{9,8},{10,9... | collective-permute-start | bytes 12296 | tf_op jit(solution)/shard_map/ppermute | solution.py:91
  321.2 6.4 %collective-permute-start.11 = (bf16[64,32]{0,1:T(8,128)(2,1)S(1)}, bf16[64,32]{0,1:T(8,128)(2,1)S(1)}, u32[]{:S(2)}, u32[]{:S(2)}) collective-permute-start(bf16[64,32]{0,1:T(8,128)(2,1)S(1)} %collective-permute-done.9), channel_id=1, source_target_pairs={{0,1},{1,2},{2,3},{3,4},{4,5},{5,6},{6,7},{7,0},{8,9},{9,10},{10,1... | collective-permute-start | bytes 12296 | tf_op jit(solution)/shard_map/ppermute | solution.py:86
  321.2 6.4 %collective-permute-start.12 = (bf16[64,32]{0,1:T(8,128)(2,1)S(1)}, bf16[64,32]{0,1:T(8,128)(2,1)S(1)}, u32[]{:S(2)}, u32[]{:S(2)}) collective-permute-start(bf16[64,32]{0,1:T(8,128)(2,1)S(1)} %collective-permute-done.10), channel_id=1, source_target_pairs={{0,7},{1,0},{2,1},{3,2},{4,3},{5,4},{6,5},{7,6},{8,15},{9,8},{10,9... | collective-permute-start | bytes 12296 | tf_op jit(solution)/shard_map/ppermute | solution.py:91
  327.6 6.3 %collective-permute-start.13 = (bf16[64,32]{0,1:T(8,128)(2,1)S(1)}, bf16[64,32]{0,1:T(8,128)(2,1)S(1)}, u32[]{:S(2)}, u32[]{:S(2)}) collective-permute-start(bf16[64,32]{0,1:T(8,128)(2,1)S(1)} %collective-permute-done.11), channel_id=1, source_target_pairs={{0,1},{1,2},{2,3},{3,4},{4,5},{5,6},{6,7},{7,0},{8,9},{9,10},{10,1... | collective-permute-start | bytes 12296 | tf_op jit(solution)/shard_map/ppermute | solution.py:86
  345.2 131.0 %all-reduce.10.cloned.1.call-start = ((), (), s32[]{:S(2)}) async-start(), calls=%async_computation.5 | async-start | bytes 262144 | tf_op jit(solution)/shard_map/psum | solution.py:11
Sparse Core Ops, SparseCore 0:
  41.1 32.7 all-reduce.7
  176.7 57.3 reduce-scatter.2
  238.0 68.8 all-reduce.11
  345.4 58.6 reduce-scatter.4
  407.3 68.8 all-reduce.9
